TPU v7x, 256 devices: a whole 4x4x8 slice. The times are simulated.
256 devices in a mesh: dp: 16 (over y_hi, z), seq: 16 (over x, y_lo, core).
Axes of the slice: x: 4, y: 4 (y_hi: 2, y_lo: 2; y = y_hi * 2 + y_lo), z: 8, core: 2. Of those that a mesh axis runs over, the one named last changes fastest.
Arguments:
- queries: bfloat16 [16, 2048, 2048], P('dp', 'seq'), may hold values from -6 to 6
- key_states: bfloat16 [16, 2048, 2048], P('dp', 'seq'), may hold values from -6 to 6
- value_states: bfloat16 [16, 2048, 2048], P('dp', 'seq'), may hold values from -6 to 6
- cotangent: bfloat16 [16, 2048, 2048], P('dp', 'seq'), may hold values from -6 to 6
- filter_taps: float32 [7, 2048], replicated, may hold values from -3 to 3
Outputs:
- conv_output: bfloat16 [16, 2048, 2048], P('dp', 'seq')
- grad_queries: bfloat16 [16, 2048, 2048], P('dp', 'seq')
- grad_keys: bfloat16 [16, 2048, 2048], P('dp', 'seq')
- grad_values: bfloat16 [16, 2048, 2048], P('dp', 'seq')
- filter_gradient: float32 [7, 2048], replicated
All inputs are finite; a program needn't handle non-finite values.
Results may differ from a plain program's by a relative error of at most 0.015.
Values may be sent and summed in bfloat16 or wider, within the bound.
No kernel may reach another device: no remote copies, remote signals or barrier semaphores. Data moves between devices by JAX's collectives and lax.ppermute only.
A program may use at most 128 MiB of HBM per device.

v0:
```python
import math
import jax
import jax.numpy as jnp
from jax import lax
from jax.sharding import PartitionSpec as P

HD = 128
TAPS = 7


def padded(value, sides, width):
    for axis, dim in sides:
        peers, length = (lax.axis_size(axis), value.shape[dim])
        up = [(i, (i + 1) % peers) for i in range(peers)]
        down = [(j, i) for i, j in up]
        last = lax.slice_in_dim(value, length - width, length, axis=dim)
        leading = lax.slice_in_dim(value, 0, width, axis=dim)
        before = lax.ppermute(last, axis, up)
        after = lax.ppermute(leading, axis, down)
        value = jnp.concatenate([before, value, after], axis=dim)
    return value


def on_device(queries, key_states, value_states, cotangent, filter_taps):
    tok_rows = queries.shape[1]
    channels = queries.shape[2]
    sequence_shards = lax.axis_size("seq")
    seq_total = tok_rows * sequence_shards
    head_count = channels // HD
    group_heads = math.gcd(head_count, 4)
    group_width = group_heads * HD
    group_count = head_count // group_heads
    score_scale = HD ** (-0.5)
    half_width = (TAPS - 1) // 2
    local_q = queries[0]
    local_k = key_states[0]
    local_v = value_states[0]
    local_g = cotangent[0]
    grad_pad = padded(local_g, (("seq", 0),), half_width)
    grad_sum = jnp.zeros((tok_rows, channels), jnp.float32)
    for tap_index in range(TAPS):
        start_row = 2 * half_width - tap_index
        grad_sum = grad_sum + filter_taps[tap_index] * grad_pad[
            start_row : start_row + tok_rows
        ].astype(jnp.float32)
    grad_attn = grad_sum.astype(jnp.bfloat16)
    key_all, value_all = (
        lax.all_gather(local_k, "seq", axis=0, tiled=True),
        lax.all_gather(local_v, "seq", axis=0, tiled=True),
    )
    device_index = lax.axis_index("seq")
    query_pos = device_index * tok_rows + jnp.arange(tok_rows, dtype=jnp.int32)
    key_pos = jnp.arange(seq_total, dtype=jnp.int32)
    visible = query_pos[:, None] >= key_pos[None, :]

    def columns(matrix, group_index, count):
        picked = lax.dynamic_slice_in_dim(matrix, group_index * group_width, group_width, 1)
        return picked.reshape(count, group_heads, HD)

    def forward_group(group_index):
        q_part = columns(local_q, group_index, tok_rows)
        k_part = columns(key_all, group_index, seq_total)
        v_part = columns(value_all, group_index, seq_total)
        delta_portion = columns(grad_attn, group_index, tok_rows)
        scores = (
            jnp.einsum("thd,uhd->htu", q_part, k_part, preferred_element_type=jnp.float32)
            * score_scale
        )
        row_top = jnp.max(jnp.where(visible, scores, -jnp.inf), -1, keepdims=True)
        raw = jnp.where(visible, jnp.exp(scores - row_top), 0.0)
        row_total = jnp.sum(raw, -1, keepdims=True)
        probs = raw / row_total
        probs_low = probs.astype(jnp.bfloat16)
        attended = jnp.einsum("htu,uhd->thd", probs_low, v_part, preferred_element_type=jnp.float32)
        attended = attended.astype(jnp.bfloat16).reshape(tok_rows, group_width)
        dprob = jnp.einsum(
            "thd,uhd->htu", delta_portion, v_part, preferred_element_type=jnp.float32
        )
        row_delta = jnp.sum(probs * dprob, -1, keepdims=True)
        dscore = (probs * (dprob - row_delta) * score_scale).astype(jnp.bfloat16)
        grad_q = jnp.einsum("htu,uhd->thd", dscore, k_part, preferred_element_type=jnp.float32)
        grad_q = grad_q.astype(jnp.bfloat16).reshape(tok_rows, group_width)
        key_term = jnp.einsum("htu,thd->uhd", dscore, q_part, preferred_element_type=jnp.float32)
        value_term = jnp.einsum(
            "htu,thd->uhd", probs_low, delta_portion, preferred_element_type=jnp.float32
        )
        return (
            attended,
            grad_q,
            key_term.reshape(seq_total, group_width),
            value_term.reshape(seq_total, group_width),
        )

    group_ids = jnp.arange(group_count, dtype=jnp.int32)
    attended, grad_q, key_term, value_term = lax.map(forward_group, group_ids)
    key_share, value_share = (
        lax.psum_scatter(
            key_term.astype(jnp.bfloat16), "seq", scatter_dimension=1, tiled=True
        ).astype(jnp.float32),
        lax.psum_scatter(
            value_term.astype(jnp.bfloat16), "seq", scatter_dimension=1, tiled=True
        ).astype(jnp.float32),
    )
    grad_keys = key_share.transpose(1, 0, 2).reshape(tok_rows, channels).astype(jnp.bfloat16)
    grad_values = value_share.transpose(1, 0, 2).reshape(tok_rows, channels).astype(jnp.bfloat16)
    attn_out = attended.transpose(1, 0, 2).reshape(tok_rows, channels)
    grad_queries = grad_q.transpose(1, 0, 2).reshape(tok_rows, channels)
    out_pad = padded(attn_out, (("seq", 0),), half_width)
    conv_sum = jnp.zeros((tok_rows, channels), jnp.float32)
    filter_rows = []
    local_gf = local_g.astype(jnp.float32)
    for tap_index in range(TAPS):
        moved = out_pad[tap_index : tap_index + tok_rows].astype(jnp.float32)
        conv_sum = conv_sum + filter_taps[tap_index] * moved
        filter_rows.append(jnp.sum(moved * local_gf, 0))
    filter_gradient = lax.psum(jnp.stack(filter_rows, 0), ("dp", "seq"))
    conv_output = conv_sum.astype(jnp.bfloat16)
    return (
        conv_output[None],
        grad_queries[None],
        grad_keys[None],
        grad_values[None],
        filter_gradient,
    )


def solution(mesh):
    in_specs = (
        P("dp", "seq", None),
        P("dp", "seq", None),
        P("dp", "seq", None),
        P("dp", "seq", None),
        P(),
    )
    out_specs = (
        P("dp", "seq", None),
        P("dp", "seq", None),
        P("dp", "seq", None),
        P("dp", "seq", None),
        P(),
    )
    return jax.shard_map(
        on_device, mesh=mesh, in_specs=in_specs, out_specs=out_specs, check_vma=False
    )
```

profile of v0, /device:TPU:1, one launch (start us, length us, event | category | flops | bytes accessed | tf_op | source)
XLA Modules:
  0.0 557.8 jit_solution(18201332075401801703)
XLA Ops:
  7.2 2.1 copy.41
  9.4 2.0 copy.43
  12.3 2.8 collective-permute-start.1
  17.1 2.0 copy.42
  19.1 1.7 fusion.47
  20.9 57.9 %all-gather.5.cloned.1.call-done = bf16[1,2048,2048]{1,2,0:T(8,128)(2,1)} async-done(((bf16[1,128,2048]{1,2,0:T(8,128)(2,1)}), bf16[1,2048,2048]{1,2,0:T(8,128)(2,1)}) %all-gather.5.cloned.1.call-update) | async-done | bytes 8388624 | tf_op jit(solution)/shard_map/all_gather | solution.py:49
  78.7 65.4 %all-gather.7.cloned.1.call-done = bf16[1,2048,2048]{1,2,0:T(8,128)(2,1)} async-done(((bf16[1,128,2048]{1,2,0:T(8,128)(2,1)}), bf16[1,2048,2048]{1,2,0:T(8,128)(2,1)}) %all-gather.7.cloned.1.call-update) | async-done | bytes 8388624 | tf_op jit(solution)/shard_map/all_gather | solution.py:48
  144.2 177.4 %while.17 = (s32[]{:T(128)}, bf16[4,128,512]{1,2,0:T(8,128)(2,1)S(1)}, bf16[4,128,512]{1,2,0:T(8,128)(2,1)}, bf16[4,2048,512]{1,2,0:T(8,128)(2,1)}, bf16[4,2048,...) while((s32[]{:T(128)}, ...), condition=%wide.region_4.5_spmd.clone, body=%wide.region_0.4_spmd.clone.sunk | while | flops 1904614400 | bytes 82324224 | solution.py:95
  145.5 3.2 constant_dynamic-slice_fusion.8
  149.7 1.7 constant_dynamic-slice_fusion.10
  151.5 2.8 fusion.110
  155.4 6.5 %fusion.111 = (f32[4,128]{1,0:T(4,128)S(1)}, f32[4,128,2048]{2,1,0:T(8,128)}) fusion(pred[128,2048]{1,0:T(8,128)(4,1)S(1)} %iota_compare_fusion.2, bf16[128,4,128]{0,2,1:T(8,128)(2,1)S(1)} %bitcast.143, bf16[2048,4,128]{0,2,1:T(8,128)(2,1)} %bitcast.125), kind=kOutput, calls=%fused_computation.95.clone.1 | convolution fusion | flops 543164416 | bytes 6686720 | tf_op jit(solution)/shard_map/while/body/eval_jaxpr/sub | solution.py:70
  161.9 8.5 %fusion.112 = bf16[4,128,128]{2,1,0:T(8,128)(2,1)S(1)} fusion(bf16[2048,4,128]{0,2,1:T(8,128)(2,1)} %bitcast.126, f32[4,128,2048]{2,1,0:T(8,128)} %fusion.110, f32[4,128,2048]{2,1,0:T(8,128)} %get-tuple-element.242, f32[4,128]{1,0:T(4,128)S(1)} %get-tuple-element.243), kind=kOutput, calls=%fused_computation.18.clone.1 | convolution fusion | flops 275843584 | bytes 10618880 | tf_op jit(solution)/shard_map/while/body/eval_jaxpr/htu,uhd->thd/dot_general | solution.py:81
  170.5 3.1 convolution_convert_fusion.2
  175.1 9.5 %fusion.114 = bf16[4,128,2048]{2,1,0:T(8,128)(2,1)} fusion(bf16[128,4,128]{0,2,1:T(8,128)(2,1)S(1)} %bitcast.144, f32[4,128,2048]{2,1,0:T(8,128)} %fusion.110, f32[4,128,2048]{2,1,0:T(8,128)} %get-tuple-element.242, f32[4,128]{1,0:T(4,128)S(1)} %get-tuple-element.243), kind=kOutput, calls=%fused_computation.10.clone.1 | convolution fusion | flops 275778048 | bytes 10618880 | tf_op jit(solution)/shard_map/while/body/eval_jaxpr/htu,thd->uhd/dot_general | solution.py:83
  184.6 4.0 constant_dynamic-update-slice_fusion.7
  189.8 3.2 constant_dynamic-slice_fusion.8
  194.1 1.7 constant_dynamic-slice_fusion.10
  195.8 2.8 fusion.110
  199.7 6.5 %fusion.111 = (f32[4,128]{1,0:T(4,128)S(1)}, f32[4,128,2048]{2,1,0:T(8,128)}) fusion(pred[128,2048]{1,0:T(8,128)(4,1)S(1)} %iota_compare_fusion.2, bf16[128,4,128]{0,2,1:T(8,128)(2,1)S(1)} %bitcast.143, bf16[2048,4,128]{0,2,1:T(8,128)(2,1)} %bitcast.125), kind=kOutput, calls=%fused_computation.95.clone.1 | convolution fusion | flops 543164416 | bytes 6686720 | tf_op jit(solution)/shard_map/while/body/eval_jaxpr/sub | solution.py:70
  206.3 8.5 %fusion.112 = bf16[4,128,128]{2,1,0:T(8,128)(2,1)S(1)} fusion(bf16[2048,4,128]{0,2,1:T(8,128)(2,1)} %bitcast.126, f32[4,128,2048]{2,1,0:T(8,128)} %fusion.110, f32[4,128,2048]{2,1,0:T(8,128)} %get-tuple-element.242, f32[4,128]{1,0:T(4,128)S(1)} %get-tuple-element.243), kind=kOutput, calls=%fused_computation.18.clone.1 | convolution fusion | flops 275843584 | bytes 10618880 | tf_op jit(solution)/shard_map/while/body/eval_jaxpr/htu,uhd->thd/dot_general | solution.py:81
  214.8 3.1 convolution_convert_fusion.2
  219.4 9.5 %fusion.114 = bf16[4,128,2048]{2,1,0:T(8,128)(2,1)} fusion(bf16[128,4,128]{0,2,1:T(8,128)(2,1)S(1)} %bitcast.144, f32[4,128,2048]{2,1,0:T(8,128)} %fusion.110, f32[4,128,2048]{2,1,0:T(8,128)} %get-tuple-element.242, f32[4,128]{1,0:T(4,128)S(1)} %get-tuple-element.243), kind=kOutput, calls=%fused_computation.10.clone.1 | convolution fusion | flops 275778048 | bytes 10618880 | tf_op jit(solution)/shard_map/while/body/eval_jaxpr/htu,thd->uhd/dot_general | solution.py:83
  228.9 4.0 constant_dynamic-update-slice_fusion.7
  234.2 3.2 constant_dynamic-slice_fusion.8
  238.4 1.7 constant_dynamic-slice_fusion.10
  240.1 2.8 fusion.110
  244.1 6.5 %fusion.111 = (f32[4,128]{1,0:T(4,128)S(1)}, f32[4,128,2048]{2,1,0:T(8,128)}) fusion(pred[128,2048]{1,0:T(8,128)(4,1)S(1)} %iota_compare_fusion.2, bf16[128,4,128]{0,2,1:T(8,128)(2,1)S(1)} %bitcast.143, bf16[2048,4,128]{0,2,1:T(8,128)(2,1)} %bitcast.125), kind=kOutput, calls=%fused_computation.95.clone.1 | convolution fusion | flops 543164416 | bytes 6686720 | tf_op jit(solution)/shard_map/while/body/eval_jaxpr/sub | solution.py:70
  250.6 8.5 %fusion.112 = bf16[4,128,128]{2,1,0:T(8,128)(2,1)S(1)} fusion(bf16[2048,4,128]{0,2,1:T(8,128)(2,1)} %bitcast.126, f32[4,128,2048]{2,1,0:T(8,128)} %fusion.110, f32[4,128,2048]{2,1,0:T(8,128)} %get-tuple-element.242, f32[4,128]{1,0:T(4,128)S(1)} %get-tuple-element.243), kind=kOutput, calls=%fused_computation.18.clone.1 | convolution fusion | flops 275843584 | bytes 10618880 | tf_op jit(solution)/shard_map/while/body/eval_jaxpr/htu,uhd->thd/dot_general | solution.py:81
  259.2 3.1 convolution_convert_fusion.2
  263.8 9.5 %fusion.114 = bf16[4,128,2048]{2,1,0:T(8,128)(2,1)} fusion(bf16[128,4,128]{0,2,1:T(8,128)(2,1)S(1)} %bitcast.144, f32[4,128,2048]{2,1,0:T(8,128)} %fusion.110, f32[4,128,2048]{2,1,0:T(8,128)} %get-tuple-element.242, f32[4,128]{1,0:T(4,128)S(1)} %get-tuple-element.243), kind=kOutput, calls=%fused_computation.10.clone.1 | convolution fusion | flops 275778048 | bytes 10618880 | tf_op jit(solution)/shard_map/while/body/eval_jaxpr/htu,thd->uhd/dot_general | solution.py:83
  273.3 4.0 constant_dynamic-update-slice_fusion.7
  278.5 3.2 constant_dynamic-slice_fusion.8
  282.7 1.7 constant_dynamic-slice_fusion.10
  284.5 2.8 fusion.110
  288.4 6.5 %fusion.111 = (f32[4,128]{1,0:T(4,128)S(1)}, f32[4,128,2048]{2,1,0:T(8,128)}) fusion(pred[128,2048]{1,0:T(8,128)(4,1)S(1)} %iota_compare_fusion.2, bf16[128,4,128]{0,2,1:T(8,128)(2,1)S(1)} %bitcast.143, bf16[2048,4,128]{0,2,1:T(8,128)(2,1)} %bitcast.125), kind=kOutput, calls=%fused_computation.95.clone.1 | convolution fusion | flops 543164416 | bytes 6686720 | tf_op jit(solution)/shard_map/while/body/eval_jaxpr/sub | solution.py:70
  294.9 8.5 %fusion.112 = bf16[4,128,128]{2,1,0:T(8,128)(2,1)S(1)} fusion(bf16[2048,4,128]{0,2,1:T(8,128)(2,1)} %bitcast.126, f32[4,128,2048]{2,1,0:T(8,128)} %fusion.110, f32[4,128,2048]{2,1,0:T(8,128)} %get-tuple-element.242, f32[4,128]{1,0:T(4,128)S(1)} %get-tuple-element.243), kind=kOutput, calls=%fused_computation.18.clone.1 | convolution fusion | flops 275843584 | bytes 10618880 | tf_op jit(solution)/shard_map/while/body/eval_jaxpr/htu,uhd->thd/dot_general | solution.py:81
  303.5 3.1 convolution_convert_fusion.2
  308.1 9.5 %fusion.114 = bf16[4,128,2048]{2,1,0:T(8,128)(2,1)} fusion(bf16[128,4,128]{0,2,1:T(8,128)(2,1)S(1)} %bitcast.144, f32[4,128,2048]{2,1,0:T(8,128)} %fusion.110, f32[4,128,2048]{2,1,0:T(8,128)} %get-tuple-element.242, f32[4,128]{1,0:T(4,128)S(1)} %get-tuple-element.243), kind=kOutput, calls=%fused_computation.10.clone.1 | convolution fusion | flops 275778048 | bytes 10618880 | tf_op jit(solution)/shard_map/while/body/eval_jaxpr/htu,thd->uhd/dot_general | solution.py:83
  317.6 4.0 constant_dynamic-update-slice_fusion.7
  321.6 14.6 %copy.60 = bf16[4,2048,512]{2,0,1:T(4,128)(2,1)} copy(bf16[4,2048,512]{1,2,0:T(8,128)(2,1)} %get-tuple-element.67) | data formatting | bytes 16777216
  336.2 10.2 %copy.65 = bf16[256,8,4,512]{3,1,2,0:T(8,128)(2,1)} copy(bf16[256,8,4,512]{3,2,1,0:T(4,128)(2,1)} %bitcast.131) | data formatting | bytes 16777216
  346.5 14.6 %copy.62 = bf16[4,2048,512]{2,0,1:T(4,128)(2,1)} copy(bf16[4,2048,512]{1,2,0:T(8,128)(2,1)} %get-tuple-element.68) | data formatting | bytes 16777216
  361.0 10.2 %copy.66 = bf16[256,8,4,512]{3,1,2,0:T(8,128)(2,1)} copy(bf16[256,8,4,512]{3,2,1,0:T(4,128)(2,1)} %bitcast.132) | data formatting | bytes 16777216
  375.9 2.0 copy.59
  379.1 78.2 %psum.7 = f32[7,2048]{1,0:T(8,128)} all-reduce(f32[7,2048]{1,0:T(8,128)S(1)} %stack.31), channel_id=1, replica_groups=mesh['dp'=16,'seq'=16] {'dp','seq'}, use_global_device_ids=true, to_apply=%region_14.15 | all-reduce | flops 14336 | bytes 114688 | tf_op jit(solution)/shard_map/psum | solution.py:116
  457.4 1.7 fusion.62
  462.0 86.5 %reduce-scatter.9.cloned.1.call-done = bf16[128,2048]{1,0:T(8,128)(2,1)} async-done(((bf16[2048,2048]{1,0:T(8,128)(2,1)}), bf16[128,2048]{1,0:T(8,128)(2,1)}) %reduce-scatter.9.cloned.1.call-update) | async-done | bytes 524304
  (107 shorter events, 31.1 us)
Async XLA Ops:
  7.2 11.9 %copy-start = (bf16[1,128,2048]{2,1,0:T(8,128)(2,1)S(1)}, bf16[1,128,2048]{2,1,0:T(8,128)(2,1)}, u32[]{:S(2)}) copy-start(bf16[1,128,2048]{2,1,0:T(8,128)(2,1)} %param.10) | copy-start | bytes 1572868
  7.2 71.6 %all-gather.5.cloned.1.call-start = ((), (), s32[]{:S(2)}) async-start(), calls=%async_computation.2 | async-start | bytes 8912896 | tf_op jit(solution)/shard_map/all_gather | solution.py:49
  9.3 134.8 %all-gather.7.cloned.1.call-start = ((), (), s32[]{:S(2)}) async-start(), calls=%async_computation.3 | async-start | bytes 8912896 | tf_op jit(solution)/shard_map/all_gather | solution.py:48
  11.5 447.6 %reduce-scatter.7.cloned.1.call-start = ((), (), s32[]{:S(2)}) async-start(), calls=%async_computation.4 | async-start | bytes 8912896
  12.3 6.8 %collective-permute-start.1 = (bf16[3,2048]{1,0:T(4,128)(2,1)S(1)}, bf16[3,2048]{1,0:T(4,128)(2,1)S(1)}, u32[]{:S(2)}, u32[]{:S(2)}) collective-permute-start(bf16[3,2048]{1,0:T(4,128)(2,1)S(1)} %get-tuple-element.161), channel_id=1, source_target_pairs={{0,1},{1,2},{2,3},{3,4},{4,5},{5,6},{6,7},{7,8},{8,9},{9,10},{10,1... | collective-permute-start | bytes 36872 | tf_op jit(solution)/shard_map/ppermute | solution.py:18
  15.1 4.0 collective-permute-start
  16.9 127.2 %copy-start.2 = (f32[1,2048]{1,0:T(1,128)}, f32[1,2048]{1,0:T(1,128)S(1)}, u32[]{:S(2)}) copy-start(f32[1,2048]{1,0:T(1,128)S(1)} %get-tuple-element.162) | copy-start | bytes 24580
  16.9 127.2 %copy-start.4 = (f32[1,2048]{1,0:T(1,128)}, f32[1,2048]{1,0:T(1,128)S(1)}, u32[]{:S(2)}) copy-start(f32[1,2048]{1,0:T(1,128)S(1)} %get-tuple-element.163) | copy-start | bytes 24580
  16.9 127.2 %copy-start.6 = (f32[1,2048]{1,0:T(1,128)}, f32[1,2048]{1,0:T(1,128)S(1)}, u32[]{:S(2)}) copy-start(f32[1,2048]{1,0:T(1,128)S(1)} %get-tuple-element.164) | copy-start | bytes 24580
  17.0 127.2 %copy-start.8 = (f32[1,2048]{1,0:T(1,128)}, f32[1,2048]{1,0:T(1,128)S(1)}, u32[]{:S(2)}) copy-start(f32[1,2048]{1,0:T(1,128)S(1)} %get-tuple-element.165) | copy-start | bytes 24580
  17.0 127.2 %copy-start.10 = (f32[1,2048]{1,0:T(1,128)}, f32[1,2048]{1,0:T(1,128)S(1)}, u32[]{:S(2)}) copy-start(f32[1,2048]{1,0:T(1,128)S(1)} %get-tuple-element.166) | copy-start | bytes 24580
  17.0 127.2 %copy-start.12 = (f32[1,2048]{1,0:T(1,128)}, f32[1,2048]{1,0:T(1,128)S(1)}, u32[]{:S(2)}) copy-start(f32[1,2048]{1,0:T(1,128)S(1)} %get-tuple-element.167) | copy-start | bytes 24580
  17.0 127.2 %copy-start.14 = (f32[1,2048]{1,0:T(1,128)}, f32[1,2048]{1,0:T(1,128)S(1)}, u32[]{:S(2)}) copy-start(f32[1,2048]{1,0:T(1,128)S(1)} %get-tuple-element.168) | copy-start | bytes 24580
  170.5 3.8 copy-start.16
  214.8 3.8 copy-start.16
  259.1 3.8 copy-start.16
  303.5 3.8 copy-start.16
  346.4 202.0 %reduce-scatter.9.cloned.1.call-start = ((), (), s32[]{:S(2)}) async-start(), calls=%async_computation.5 | async-start | bytes 8912896
  371.3 1.0 copy-start.1
  372.5 84.8 %copy-start.3 = (f32[1,2048]{1,0:T(1,128)S(1)}, f32[1,2048]{1,0:T(1,128)}, u32[]{:S(2)}) copy-start(f32[1,2048]{1,0:T(1,128)} %copy-done.2) | copy-start | bytes 24580
  372.5 84.8 %copy-start.5 = (f32[1,2048]{1,0:T(1,128)S(1)}, f32[1,2048]{1,0:T(1,128)}, u32[]{:S(2)}) copy-start(f32[1,2048]{1,0:T(1,128)} %copy-done.4) | copy-start | bytes 24580
  372.6 84.8 %copy-start.7 = (f32[1,2048]{1,0:T(1,128)S(1)}, f32[1,2048]{1,0:T(1,128)}, u32[]{:S(2)}) copy-start(f32[1,2048]{1,0:T(1,128)} %copy-done.6) | copy-start | bytes 24580
  372.6 84.7 %copy-start.9 = (f32[1,2048]{1,0:T(1,128)S(1)}, f32[1,2048]{1,0:T(1,128)}, u32[]{:S(2)}) copy-start(f32[1,2048]{1,0:T(1,128)} %copy-done.8) | copy-start | bytes 24580
  372.6 84.7 %copy-start.11 = (f32[1,2048]{1,0:T(1,128)S(1)}, f32[1,2048]{1,0:T(1,128)}, u32[]{:S(2)}) copy-start(f32[1,2048]{1,0:T(1,128)} %copy-done.10) | copy-start | bytes 24580
  372.6 84.7 %copy-start.13 = (f32[1,2048]{1,0:T(1,128)S(1)}, f32[1,2048]{1,0:T(1,128)}, u32[]{:S(2)}) copy-start(f32[1,2048]{1,0:T(1,128)} %copy-done.12) | copy-start | bytes 24580
  372.6 84.7 %copy-start.15 = (f32[1,2048]{1,0:T(1,128)S(1)}, f32[1,2048]{1,0:T(1,128)}, u32[]{:S(2)}) copy-start(f32[1,2048]{1,0:T(1,128)} %copy-done.14) | copy-start | bytes 24580
  373.0 4.9 collective-permute-start.3
  373.7 4.3 collective-permute-start.2
Sparse Core Ops, SparseCore 0:
  10.4 68.3 all-gather.4
  81.1 63.0 all-gather.6
  346.6 99.6 reduce-scatter.6
  448.7 99.6 reduce-scatter.8
where the time goes:
time: 560 us; the launch traced here: 558 us
  waiting for transfers between devices  210 us (38%)
  matrix products  125 us (22%)
  local copies, waits for them, and re-layouts  116 us (21%)
  blocking collectives  78.2 us (14%)
  between operations  14.1 us (3%)
  other arithmetic  5.7 us (1%)
  starting transfers between devices  5.66 us (1%)
    unnamed x6, waiting for transfers between devices  86.6 us
    psum x1, blocking collectives, on_device(): filter_gradient = lax.psum(jnp.stack(filter_rows, 0), ('dp', 'seq'))  78.2 us
    all_gather x1, waiting for transfers between devices, on_device(): lax.all_gather(local_k, 'seq', axis=0, tiled=True)  65.4 us
    unnamed x46, local copies, waits for them, and re-layouts  62.6 us
    all_gather x1, waiting for transfers between devices, on_device(): lax.all_gather(local_v, 'seq', axis=0, tiled=True)  57.9 us
    dot_general x4, matrix products, forward_group(): jnp.einsum('htu,thd->uhd', dscore, q_part, preferred_element_type=jnp.flo...  38 us
    dot_general x4, matrix products, forward_group(): jnp.einsum('htu,uhd->thd', dscore, k_part, preferred_element_type=jnp.flo...  34.2 us
    dynamic_slice x20, local copies, waits for them, and re-layouts, columns(): lax.dynamic_slice_in_dim(matrix, group_index * group_width, group_width, 1)  27.5 us
  transfers between devices with their start and end apart: 8, of which 3 were waited for; matrix products, arithmetic and copies ran while one was open for 7% of the time, Pallas kernels for 0%

commit v1 on v0

--- a/solution.py
+++ b/solution.py
@@ -1,3 +1,4 @@
+import functools
 import math
 import jax
 import jax.numpy as jnp
@@ -6,6 +7,15 @@
 
 HD = 128
 TAPS = 7
+
+
+def answer_terms(message, dim_k):
+    return jnp.concatenate(
+        lax.all_to_all(jnp.stack(lax.axis_size("seq") * [message]), "seq", 0, 0), axis=dim_k
+    )
+
+
+levels_all_render = functools.partial(answer_terms, dim_k=0)
 
 
 def padded(value, sides, width):
@@ -46,7 +56,7 @@
     grad_attn = grad_sum.astype(jnp.bfloat16)
     key_all, value_all = (
         lax.all_gather(local_k, "seq", axis=0, tiled=True),
-        lax.all_gather(local_v, "seq", axis=0, tiled=True),
+        levels_all_render(local_v),
     )
     device_index = lax.axis_index("seq")
     query_pos = device_index * tok_rows + jnp.arange(tok_rows, dtype=jnp.int32)

time: 560 us -> 623 us (1.11)
  local copies, waits for them, and re-layouts: 116 us -> 147 us
  waiting for transfers between devices: 210 us -> 227 us
  starting transfers between devices: 5.66 us -> 19 us
    ppermute x2, waiting for transfers between devices: 0.01 us -> 78 us  [padded(): before = lax.ppermute(last, axis, up)]
    all_gather x1, waiting for transfers between devices: 65.4 us -> 1.21 us  [on_device(): lax.all_gather(local_k, 'seq', axis=0, tiled=True)]
    all_gather x1 -> x0, waiting for transfers between devices: 57.9 us -> none  [on_device(): lax.all_gather(local_v, 'seq', axis=0, tiled=True)]
    all_to_all x0 -> x1, waiting for transfers between devices: none -> 48.8 us  [answer_terms(): lax.all_to_all(jnp.stack(lax.axis_size('seq') * [message]), 'seq', 0, 0)]
    dynamic_slice x20 -> x24, local copies, waits for them, and re-layouts: 27.5 us -> 44.6 us  [columns(): lax.dynamic_slice_in_dim(matrix, group_index * group_width, group_width, 1)]
    all_to_all x0 -> x1, local copies, waits for them, and re-layouts: none -> 12.3 us  [answer_terms(): lax.all_to_all(jnp.stack(lax.axis_size('seq') * [message]), 'seq', 0, 0)]
    ppermute x2, waiting for transfers between devices: 0.01 us -> 10.6 us  [padded(): after = lax.ppermute(leading, axis, down)]
    all_to_all x0 -> x1, starting transfers between devices: none -> 7.83 us  [answer_terms(): lax.all_to_all(jnp.stack(lax.axis_size('seq') * [message]), 'seq', 0, 0)]
  transfers between devices with their start and end apart: 8 -> 8, of which waited for: 3 -> 5; matrix products, arithmetic and copies ran while one was open for 7% -> 9% of each run, Pallas kernels for 0% -> 0%
where the time goes in v1:
time: 623 us; the launch traced here: 620 us
  waiting for transfers between devices  227 us (36%)
  local copies, waits for them, and re-layouts  147 us (24%)
  matrix products  125 us (20%)
  blocking collectives  79.8 us (13%)
  starting transfers between devices  19 us (3%)
  between operations  14.1 us (2%)
    unnamed x5, waiting for transfers between devices  88.7 us
    psum x1, blocking collectives, on_device(): filter_gradient = lax.psum(jnp.stack(filter_rows, 0), ('dp', 'seq'))  79.8 us
    ppermute x2, waiting for transfers between devices, padded(): before = lax.ppermute(last, axis, up)  78 us
    unnamed x49, local copies, waits for them, and re-layouts  59.4 us
    all_to_all x1, waiting for transfers between devices, answer_terms(): lax.all_to_all(jnp.stack(lax.axis_size('seq') * [message]), 'seq', 0, 0)  48.8 us
    dynamic_slice x24, local copies, waits for them, and re-layouts, columns(): lax.dynamic_slice_in_dim(matrix, group_index * group_width, group_width, 1)  44.6 us
    dot_general x4, matrix products, forward_group(): jnp.einsum('htu,thd->uhd', dscore, q_part, preferred_element_type=jnp.flo...  38 us
    dot_general x4, matrix products, forward_group(): jnp.einsum('htu,uhd->thd', dscore, k_part, preferred_element_type=jnp.flo...  34.2 us
  transfers between devices with their start and end apart: 8, of which 5 were waited for; matrix products, arithmetic and copies ran while one was open for 9% of the time, Pallas kernels for 0%

profile of v1, /device:TPU:1, one launch (start us, length us, event | category | flops | bytes accessed | tf_op | source)
XLA Modules:
  0.0 620.4 jit_solution(13969768179911156888)
XLA Ops:
  10.6 4.8 stack.27
  15.4 7.8 %all-to-all-start = ((bf16[16,128,2048]{1,2,0:T(8,128)(2,1)}), bf16[16,128,2048]{1,2,0:T(8,128)(2,1)}, u32[]{:S(2)}, u32[]{:S(2)}) async-start(bf16[16,128,2048]{1,2,0:T(8,128)(2,1)} %stack.27), calls=%async_computation | async-start | bytes 16777216 | tf_op jit(solution)/shard_map/all_to_all | solution.py:14
  26.2 78.0 %collective-permute-done.1 = bf16[3,2048]{1,0:T(4,128)(2,1)S(1)} collective-permute-done((bf16[3,2048]{1,0:T(4,128)(2,1)S(1)}, bf16[3,2048]{1,0:T(4,128)(2,1)S(1)}, u32[]{:S(2)}, u32[]{:S(2)}) %collective-permute-start.1) | collective-permute-done | bytes 12320 | tf_op jit(solution)/shard_map/ppermute | solution.py:28
  104.3 10.6 %collective-permute-done = bf16[3,2048]{1,0:T(4,128)(2,1)S(1)} collective-permute-done((bf16[3,2048]{1,0:T(4,128)(2,1)S(1)}, bf16[3,2048]{1,0:T(4,128)(2,1)S(1)}, u32[]{:S(2)}, u32[]{:S(2)}) %collective-permute-start) | collective-permute-done | bytes 12320 | tf_op jit(solution)/shard_map/ppermute | solution.py:29
  116.6 48.8 %all-to-all-done = bf16[16,128,2048]{1,2,0:T(8,128)(2,1)} async-done(((bf16[16,128,2048]{1,2,0:T(8,128)(2,1)}), bf16[16,128,2048]{1,2,0:T(8,128)(2,1)}, u32[]{:S(2)}, u32[]{:S(2)}) %all-to-all-start) | async-done | bytes 8388640 | tf_op jit(solution)/shard_map/all_to_all | solution.py:14
  165.4 12.3 %copy.57 = bf16[16,128,2048]{2,1,0:T(8,128)(2,1)} copy(bf16[16,128,2048]{1,2,0:T(8,128)(2,1)} %all-to-all-done) | data formatting | bytes 16777216 | tf_op jit(solution)/shard_map/all_to_all | solution.py:14
  179.0 194.3 %while.17 = (s32[]{:T(128)}, bf16[4,128,512]{1,2,0:T(8,128)(2,1)S(1)}, bf16[4,128,512]{1,2,0:T(8,128)(2,1)}, bf16[4,2048,512]{1,2,0:T(8,128)(2,1)}, bf16[4,2048,...) while((s32[]{:T(128)}, ...), condition=%wide.region_4.5_spmd.clone, body=%wide.region_0.4_spmd.clone.sunk | while | flops 1904614400 | bytes 86518528 | solution.py:105
  180.2 3.2 constant_dynamic-slice_fusion.8
  184.5 3.1 constant_dynamic-slice_fusion.10
  187.6 2.9 copy.89
  190.5 2.7 fusion.110
  194.3 6.5 %fusion.111 = (f32[4,128]{1,0:T(4,128)S(1)}, f32[4,128,2048]{2,1,0:T(8,128)}) fusion(pred[128,2048]{1,0:T(8,128)(4,1)S(1)} %iota_compare_fusion.2, bf16[128,4,128]{0,2,1:T(8,128)(2,1)S(1)} %bitcast.144, bf16[2048,4,128]{0,2,1:T(8,128)(2,1)} %bitcast.126), kind=kOutput, calls=%fused_computation.95.clone.1 | convolution fusion | flops 543164416 | bytes 6686720 | tf_op jit(solution)/shard_map/while/body/eval_jaxpr/sub | solution.py:80
  200.9 8.5 %fusion.112 = bf16[4,128,128]{2,1,0:T(8,128)(2,1)S(1)} fusion(bf16[2048,4,128]{0,2,1:T(8,128)(2,1)} %bitcast.127, f32[4,128,2048]{2,1,0:T(8,128)} %fusion.110, f32[4,128,2048]{2,1,0:T(8,128)} %get-tuple-element.258, f32[4,128]{1,0:T(4,128)S(1)} %get-tuple-element.259), kind=kOutput, calls=%fused_computation.18.clone.1 | convolution fusion | flops 275843584 | bytes 10618880 | tf_op jit(solution)/shard_map/while/body/eval_jaxpr/htu,uhd->thd/dot_general | solution.py:91
  209.4 3.1 convolution_convert_fusion.2
  214.0 9.5 %fusion.114 = bf16[4,128,2048]{2,1,0:T(8,128)(2,1)} fusion(bf16[128,4,128]{0,2,1:T(8,128)(2,1)S(1)} %bitcast.145, f32[4,128,2048]{2,1,0:T(8,128)} %fusion.110, f32[4,128,2048]{2,1,0:T(8,128)} %get-tuple-element.258, f32[4,128]{1,0:T(4,128)S(1)} %get-tuple-element.259), kind=kOutput, calls=%fused_computation.10.clone.1 | convolution fusion | flops 275778048 | bytes 10618880 | tf_op jit(solution)/shard_map/while/body/eval_jaxpr/htu,thd->uhd/dot_general | solution.py:93
  223.5 4.1 constant_dynamic-update-slice_fusion.7
  228.9 3.2 constant_dynamic-slice_fusion.8
  233.2 3.1 constant_dynamic-slice_fusion.10
  236.2 2.9 copy.89
  239.2 2.7 fusion.110
  243.0 6.5 %fusion.111 = (f32[4,128]{1,0:T(4,128)S(1)}, f32[4,128,2048]{2,1,0:T(8,128)}) fusion(pred[128,2048]{1,0:T(8,128)(4,1)S(1)} %iota_compare_fusion.2, bf16[128,4,128]{0,2,1:T(8,128)(2,1)S(1)} %bitcast.144, bf16[2048,4,128]{0,2,1:T(8,128)(2,1)} %bitcast.126), kind=kOutput, calls=%fused_computation.95.clone.1 | convolution fusion | flops 543164416 | bytes 6686720 | tf_op jit(solution)/shard_map/while/body/eval_jaxpr/sub | solution.py:80
  249.5 8.5 %fusion.112 = bf16[4,128,128]{2,1,0:T(8,128)(2,1)S(1)} fusion(bf16[2048,4,128]{0,2,1:T(8,128)(2,1)} %bitcast.127, f32[4,128,2048]{2,1,0:T(8,128)} %fusion.110, f32[4,128,2048]{2,1,0:T(8,128)} %get-tuple-element.258, f32[4,128]{1,0:T(4,128)S(1)} %get-tuple-element.259), kind=kOutput, calls=%fused_computation.18.clone.1 | convolution fusion | flops 275843584 | bytes 10618880 | tf_op jit(solution)/shard_map/while/body/eval_jaxpr/htu,uhd->thd/dot_general | solution.py:91
  258.1 3.1 convolution_convert_fusion.2
  262.7 9.5 %fusion.114 = bf16[4,128,2048]{2,1,0:T(8,128)(2,1)} fusion(bf16[128,4,128]{0,2,1:T(8,128)(2,1)S(1)} %bitcast.145, f32[4,128,2048]{2,1,0:T(8,128)} %fusion.110, f32[4,128,2048]{2,1,0:T(8,128)} %get-tuple-element.258, f32[4,128]{1,0:T(4,128)S(1)} %get-tuple-element.259), kind=kOutput, calls=%fused_computation.10.clone.1 | convolution fusion | flops 275778048 | bytes 10618880 | tf_op jit(solution)/shard_map/while/body/eval_jaxpr/htu,thd->uhd/dot_general | solution.py:93
  272.2 4.0 constant_dynamic-update-slice_fusion.7
  277.4 3.2 constant_dynamic-slice_fusion.8
  281.6 3.1 constant_dynamic-slice_fusion.10
  284.7 2.9 copy.89
  291.5 6.5 %fusion.111 = (f32[4,128]{1,0:T(4,128)S(1)}, f32[4,128,2048]{2,1,0:T(8,128)}) fusion(pred[128,2048]{1,0:T(8,128)(4,1)S(1)} %iota_compare_fusion.2, bf16[128,4,128]{0,2,1:T(8,128)(2,1)S(1)} %bitcast.144, bf16[2048,4,128]{0,2,1:T(8,128)(2,1)} %bitcast.126), kind=kOutput, calls=%fused_computation.95.clone.1 | convolution fusion | flops 543164416 | bytes 6686720 | tf_op jit(solution)/shard_map/while/body/eval_jaxpr/sub | solution.py:80
  298.0 8.5 %fusion.112 = bf16[4,128,128]{2,1,0:T(8,128)(2,1)S(1)} fusion(bf16[2048,4,128]{0,2,1:T(8,128)(2,1)} %bitcast.127, f32[4,128,2048]{2,1,0:T(8,128)} %fusion.110, f32[4,128,2048]{2,1,0:T(8,128)} %get-tuple-element.258, f32[4,128]{1,0:T(4,128)S(1)} %get-tuple-element.259), kind=kOutput, calls=%fused_computation.18.clone.1 | convolution fusion | flops 275843584 | bytes 10618880 | tf_op jit(solution)/shard_map/while/body/eval_jaxpr/htu,uhd->thd/dot_general | solution.py:91
  306.6 3.1 convolution_convert_fusion.2
  311.2 9.5 %fusion.114 = bf16[4,128,2048]{2,1,0:T(8,128)(2,1)} fusion(bf16[128,4,128]{0,2,1:T(8,128)(2,1)S(1)} %bitcast.145, f32[4,128,2048]{2,1,0:T(8,128)} %fusion.110, f32[4,128,2048]{2,1,0:T(8,128)} %get-tuple-element.258, f32[4,128]{1,0:T(4,128)S(1)} %get-tuple-element.259), kind=kOutput, calls=%fused_computation.10.clone.1 | convolution fusion | flops 275778048 | bytes 10618880 | tf_op jit(solution)/shard_map/while/body/eval_jaxpr/htu,thd->uhd/dot_general | solution.py:93
  320.7 4.1 constant_dynamic-update-slice_fusion.7
  326.0 3.2 constant_dynamic-slice_fusion.8
  330.2 3.1 constant_dynamic-slice_fusion.10
  333.3 2.9 copy.89
  340.1 6.5 %fusion.111 = (f32[4,128]{1,0:T(4,128)S(1)}, f32[4,128,2048]{2,1,0:T(8,128)}) fusion(pred[128,2048]{1,0:T(8,128)(4,1)S(1)} %iota_compare_fusion.2, bf16[128,4,128]{0,2,1:T(8,128)(2,1)S(1)} %bitcast.144, bf16[2048,4,128]{0,2,1:T(8,128)(2,1)} %bitcast.126), kind=kOutput, calls=%fused_computation.95.clone.1 | convolution fusion | flops 543164416 | bytes 6686720 | tf_op jit(solution)/shard_map/while/body/eval_jaxpr/sub | solution.py:80
  346.6 8.5 %fusion.112 = bf16[4,128,128]{2,1,0:T(8,128)(2,1)S(1)} fusion(bf16[2048,4,128]{0,2,1:T(8,128)(2,1)} %bitcast.127, f32[4,128,2048]{2,1,0:T(8,128)} %fusion.110, f32[4,128,2048]{2,1,0:T(8,128)} %get-tuple-element.258, f32[4,128]{1,0:T(4,128)S(1)} %get-tuple-element.259), kind=kOutput, calls=%fused_computation.18.clone.1 | convolution fusion | flops 275843584 | bytes 10618880 | tf_op jit(solution)/shard_map/while/body/eval_jaxpr/htu,uhd->thd/dot_general | solution.py:91
  355.2 3.1 convolution_convert_fusion.2
  359.8 9.5 %fusion.114 = bf16[4,128,2048]{2,1,0:T(8,128)(2,1)} fusion(bf16[128,4,128]{0,2,1:T(8,128)(2,1)S(1)} %bitcast.145, f32[4,128,2048]{2,1,0:T(8,128)} %fusion.110, f32[4,128,2048]{2,1,0:T(8,128)} %get-tuple-element.258, f32[4,128]{1,0:T(4,128)S(1)} %get-tuple-element.259), kind=kOutput, calls=%fused_computation.10.clone.1 | convolution fusion | flops 275778048 | bytes 10618880 | tf_op jit(solution)/shard_map/while/body/eval_jaxpr/htu,thd->uhd/dot_general | solution.py:93
  369.3 4.0 constant_dynamic-update-slice_fusion.7
  373.3 14.6 %copy.77 = bf16[4,2048,512]{2,0,1:T(4,128)(2,1)} copy(bf16[4,2048,512]{1,2,0:T(8,128)(2,1)} %get-tuple-element.67) | data formatting | bytes 16777216
  387.9 10.2 %copy.83 = bf16[256,8,4,512]{3,1,2,0:T(8,128)(2,1)} copy(bf16[256,8,4,512]{3,2,1,0:T(4,128)(2,1)} %bitcast.133) | data formatting | bytes 16777216
  398.1 14.5 %copy.79 = bf16[4,2048,512]{2,0,1:T(4,128)(2,1)} copy(bf16[4,2048,512]{1,2,0:T(8,128)(2,1)} %get-tuple-element.68) | data formatting | bytes 16777216
  412.7 10.2 %copy.84 = bf16[256,8,4,512]{3,1,2,0:T(8,128)(2,1)} copy(bf16[256,8,4,512]{3,2,1,0:T(4,128)(2,1)} %bitcast.134) | data formatting | bytes 16777216
  425.3 8.8 %collective-permute-start.2 = (bf16[3,2048]{1,0:T(4,128)(2,1)S(1)}, bf16[3,2048]{1,0:T(4,128)(2,1)S(1)}, u32[]{:S(2)}, u32[]{:S(2)}) collective-permute-start(bf16[3,2048]{1,0:T(4,128)(2,1)S(1)} %copy.73), channel_id=1, source_target_pairs={{0,1},{1,2},{2,3},{3,4},{4,5},{5,6},{6,7},{7,8},{8,9},{9,10},{10,1... | collective-permute-start | bytes 36872 | tf_op jit(solution)/shard_map/ppermute | solution.py:28
  437.9 79.8 %psum.7 = f32[7,2048]{1,0:T(8,128)} all-reduce(f32[7,2048]{1,0:T(8,128)S(1)} %stack.35), channel_id=1, replica_groups=mesh['dp'=16,'seq'=16] {'dp','seq'}, use_global_device_ids=true, to_apply=%region_14.15 | all-reduce | flops 14336 | bytes 114688 | tf_op jit(solution)/shard_map/psum | solution.py:126
  522.4 88.7 %reduce-scatter.9.cloned.1.call-done = bf16[128,2048]{1,0:T(8,128)(2,1)} async-done(((bf16[2048,2048]{1,0:T(8,128)(2,1)}), bf16[128,2048]{1,0:T(8,128)(2,1)}) %reduce-scatter.9.cloned.1.call-update) | async-done | bytes 524304
  (116 shorter events, 45.1 us)
Async XLA Ops:
  7.2 171.8 %all-gather.3.cloned.1.call-start = ((), (), s32[]{:S(2)}) async-start(), calls=%async_computation.3 | async-start | bytes 8912896 | tf_op jit(solution)/shard_map/all_gather | solution.py:58
  15.4 7.9 %copy-start = (bf16[1,128,2048]{2,1,0:T(8,128)(2,1)S(1)}, bf16[1,128,2048]{2,1,0:T(8,128)(2,1)}, u32[]{:S(2)}) copy-start(bf16[1,128,2048]{2,1,0:T(8,128)(2,1)} %param.10) | copy-start | bytes 1572868
  15.4 9.6 %copy-start.17 = (f32[7,2048]{1,0:T(8,128)S(1)}, f32[7,2048]{1,0:T(8,128)}, u32[]{:S(2)}) copy-start(f32[7,2048]{1,0:T(8,128)} %param.11) | copy-start | bytes 172036
  15.4 9.8 %copy-start.2 = (bf16[1,128,2048]{2,1,0:T(8,128)(2,1)S(1)}, bf16[1,128,2048]{2,1,0:T(8,128)(2,1)}, u32[]{:S(2)}) copy-start(bf16[1,128,2048]{2,1,0:T(8,128)(2,1)} %param.7) | copy-start | bytes 1572868
  15.4 150.0 %all-to-all-start = ((bf16[16,128,2048]{1,2,0:T(8,128)(2,1)}), bf16[16,128,2048]{1,2,0:T(8,128)(2,1)}, u32[]{:S(2)}, u32[]{:S(2)}) async-start(bf16[16,128,2048]{1,2,0:T(8,128)(2,1)} %stack.27), calls=%async_computation | async-start | bytes 16777216 | tf_op jit(solution)/shard_map/all_to_all | solution.py:14
  23.3 496.2 %reduce-scatter.7.cloned.1.call-start = ((), (), s32[]{:S(2)}) async-start(), calls=%async_computation.4 | async-start | bytes 8912896
  23.3 80.9 %collective-permute-start.1 = (bf16[3,2048]{1,0:T(4,128)(2,1)S(1)}, bf16[3,2048]{1,0:T(4,128)(2,1)S(1)}, u32[]{:S(2)}, u32[]{:S(2)}) collective-permute-start(bf16[3,2048]{1,0:T(4,128)(2,1)S(1)} %get-tuple-element.177), channel_id=1, source_target_pairs={{0,1},{1,2},{2,3},{3,4},{4,5},{5,6},{6,7},{7,8},{8,9},{9,10},{10,1... | collective-permute-start | bytes 36872 | tf_op jit(solution)/shard_map/ppermute | solution.py:28
  25.1 89.8 %collective-permute-start = (bf16[3,2048]{1,0:T(4,128)(2,1)S(1)}, bf16[3,2048]{1,0:T(4,128)(2,1)S(1)}, u32[]{:S(2)}, u32[]{:S(2)}) collective-permute-start(bf16[3,2048]{1,0:T(4,128)(2,1)S(1)} %get-tuple-element.176), channel_id=1, source_target_pairs={{1,0},{2,1},{3,2},{4,3},{5,4},{6,5},{7,6},{8,7},{9,8},{10,9},{11,1... | collective-permute-start | bytes 36872 | tf_op jit(solution)/shard_map/ppermute | solution.py:29
  25.1 152.6 %copy-start.3 = (f32[1,2048]{1,0:T(1,128)}, f32[1,2048]{1,0:T(1,128)S(1)}, u32[]{:S(2)}) copy-start(f32[1,2048]{1,0:T(1,128)S(1)} %get-tuple-element.178) | copy-start | bytes 24580
  25.1 152.6 %copy-start.5 = (f32[1,2048]{1,0:T(1,128)}, f32[1,2048]{1,0:T(1,128)S(1)}, u32[]{:S(2)}) copy-start(f32[1,2048]{1,0:T(1,128)S(1)} %get-tuple-element.179) | copy-start | bytes 24580
  25.1 152.6 %copy-start.7 = (f32[1,2048]{1,0:T(1,128)}, f32[1,2048]{1,0:T(1,128)S(1)}, u32[]{:S(2)}) copy-start(f32[1,2048]{1,0:T(1,128)S(1)} %get-tuple-element.180) | copy-start | bytes 24580
  25.1 152.6 %copy-start.9 = (f32[1,2048]{1,0:T(1,128)}, f32[1,2048]{1,0:T(1,128)S(1)}, u32[]{:S(2)}) copy-start(f32[1,2048]{1,0:T(1,128)S(1)} %get-tuple-element.181) | copy-start | bytes 24580
  25.2 152.6 %copy-start.11 = (f32[1,2048]{1,0:T(1,128)}, f32[1,2048]{1,0:T(1,128)S(1)}, u32[]{:S(2)}) copy-start(f32[1,2048]{1,0:T(1,128)S(1)} %get-tuple-element.182) | copy-start | bytes 24580
  25.2 152.6 %copy-start.13 = (f32[1,2048]{1,0:T(1,128)}, f32[1,2048]{1,0:T(1,128)S(1)}, u32[]{:S(2)}) copy-start(f32[1,2048]{1,0:T(1,128)S(1)} %get-tuple-element.183) | copy-start | bytes 24580
  25.2 152.6 %copy-start.15 = (f32[1,2048]{1,0:T(1,128)}, f32[1,2048]{1,0:T(1,128)S(1)}, u32[]{:S(2)}) copy-start(f32[1,2048]{1,0:T(1,128)S(1)} %get-tuple-element.184) | copy-start | bytes 24580
  209.4 3.8 copy-start.18
  258.1 3.8 copy-start.18
  306.6 3.8 copy-start.18
  355.2 3.8 copy-start.18
  398.1 212.9 %reduce-scatter.9.cloned.1.call-start = ((), (), s32[]{:S(2)}) async-start(), calls=%async_computation.5 | async-start | bytes 8912896
  422.9 1.1 copy-start.1
  424.1 93.6 %copy-start.4 = (f32[1,2048]{1,0:T(1,128)S(1)}, f32[1,2048]{1,0:T(1,128)}, u32[]{:S(2)}) copy-start(f32[1,2048]{1,0:T(1,128)} %copy-done.3) | copy-start | bytes 24580
  424.2 93.5 %copy-start.6 = (f32[1,2048]{1,0:T(1,128)S(1)}, f32[1,2048]{1,0:T(1,128)}, u32[]{:S(2)}) copy-start(f32[1,2048]{1,0:T(1,128)} %copy-done.5) | copy-start | bytes 24580
  424.2 93.5 %copy-start.8 = (f32[1,2048]{1,0:T(1,128)S(1)}, f32[1,2048]{1,0:T(1,128)}, u32[]{:S(2)}) copy-start(f32[1,2048]{1,0:T(1,128)} %copy-done.7) | copy-start | bytes 24580
  424.2 93.5 %copy-start.10 = (f32[1,2048]{1,0:T(1,128)S(1)}, f32[1,2048]{1,0:T(1,128)}, u32[]{:S(2)}) copy-start(f32[1,2048]{1,0:T(1,128)} %copy-done.9) | copy-start | bytes 24580
  424.2 93.5 %copy-start.12 = (f32[1,2048]{1,0:T(1,128)S(1)}, f32[1,2048]{1,0:T(1,128)}, u32[]{:S(2)}) copy-start(f32[1,2048]{1,0:T(1,128)} %copy-done.11) | copy-start | bytes 24580
  424.2 93.5 %copy-start.14 = (f32[1,2048]{1,0:T(1,128)S(1)}, f32[1,2048]{1,0:T(1,128)}, u32[]{:S(2)}) copy-start(f32[1,2048]{1,0:T(1,128)} %copy-done.13) | copy-start | bytes 24580
  424.2 93.5 %copy-start.16 = (f32[1,2048]{1,0:T(1,128)S(1)}, f32[1,2048]{1,0:T(1,128)}, u32[]{:S(2)}) copy-start(f32[1,2048]{1,0:T(1,128)} %copy-done.15) | copy-start | bytes 24580
  424.7 12.2 %collective-permute-start.3 = (bf16[3,2048]{1,0:T(4,128)(2,1)S(1)}, bf16[3,2048]{1,0:T(4,128)(2,1)S(1)}, u32[]{:S(2)}, u32[]{:S(2)}) collective-permute-start(bf16[3,2048]{1,0:T(4,128)(2,1)S(1)} %copy.75), channel_id=1, source_target_pairs={{1,0},{2,1},{3,2},{4,3},{5,4},{6,5},{7,6},{8,7},{9,8},{10,9},{11,1... | collective-permute-start | bytes 36872 | tf_op jit(solution)/shard_map/ppermute | solution.py:29
  425.3 11.5 %collective-permute-start.2 = (bf16[3,2048]{1,0:T(4,128)(2,1)S(1)}, bf16[3,2048]{1,0:T(4,128)(2,1)S(1)}, u32[]{:S(2)}, u32[]{:S(2)}) collective-permute-start(bf16[3,2048]{1,0:T(4,128)(2,1)S(1)} %copy.73), channel_id=1, source_target_pairs={{0,1},{1,2},{2,3},{3,4},{4,5},{5,6},{6,7},{7,8},{8,9},{9,10},{10,1... | collective-permute-start | bytes 36872 | tf_op jit(solution)/shard_map/ppermute | solution.py:28
Sparse Core Ops, SparseCore 0:
  10.3 168.6 all-gather.2
  398.2 109.7 reduce-scatter.6
  510.6 100.3 reduce-scatter.8
